TPU v7x, 256 devices: a whole 4x4x8 slice. The times are simulated.
256 devices in a mesh: seq: 128 (over x, y, z_lo, core), dp: 2 (over z_hi).
Axes of the slice: x: 4, y: 4, z: 8 (z_hi: 2, z_lo: 4; z = z_hi * 4 + z_lo), core: 2. Of those that a mesh axis runs over, the one named last changes fastest.
Arguments:
- inputs: bfloat16 [2, 256, 256, 512], P('dp', 'seq'), may hold values from -6 to 6
- gate: bfloat16 [2, 256, 256, 512], P('dp', 'seq'), may hold values from -6 to 6
- kernel: bfloat16 [256, 256, 512], P(None, 'seq'), may hold values from -6 to 6
- first_blocks: bfloat16 [256, 256, 256], P('seq'), may hold values from -0.375 to 0.375
- second_blocks: bfloat16 [256, 256, 256], P('seq'), may hold values from -0.375 to 0.375
- cotangent: bfloat16 [2, 256, 256, 512], P('dp', 'seq'), may hold values from -6 to 6
Outputs:
- mixed: bfloat16 [2, 256, 256, 512], P('dp', 'seq')
- grad_inputs: bfloat16 [2, 256, 256, 512], P('dp', 'seq')
- grad_gate: bfloat16 [2, 256, 256, 512], P('dp', 'seq')
- grad_kernel: float32 [256, 256, 512], P(None, 'seq')
All inputs are finite; a program needn't handle non-finite values.
Results may differ from a plain program's by a relative error of at most 0.007.
Values may be sent and summed in bfloat16 or wider, within the bound.
No kernel may reach another device: no remote copies, remote signals or barrier semaphores. Data moves between devices by JAX's collectives and lax.ppermute only.
A program may use at most 64 MiB of HBM per device.

v0:
```python
import jax
import jax.numpy as jnp
from jax import lax
from jax.sharding import PartitionSpec as P


def shards(inputs, gate, kernel, first_blocks, second_blocks, cotangent):
    f32 = jnp.float32
    bf16 = jnp.bfloat16
    gate32 = gate.astype(f32)
    cot = cotangent.astype(f32)
    d_result = (cot * gate32).astype(bf16)

    def spread(rows):
        return jnp.einsum("rij,srjd->srid", first_blocks, rows, preferred_element_type=f32).astype(
            bf16
        )

    def mix_columns(piece):
        return jnp.einsum("cqr,srcd->sqcd", second_blocks, piece, preferred_element_type=f32)

    def unmix_columns(scaled):
        return jnp.einsum(
            "cqr,sqcd->srcd", second_blocks, scaled, preferred_element_type=f32
        ).astype(bf16)

    def finish_rows(piece):
        return jnp.einsum("rij,srid->srjd", first_blocks, piece, preferred_element_type=f32)

    second = mix_columns(
        lax.all_to_all(spread(inputs), "seq", split_axis=2, concat_axis=1, tiled=True)
    )
    hidden = (second * kernel).astype(bf16)
    result = finish_rows(
        lax.all_to_all(unmix_columns(hidden), "seq", split_axis=1, concat_axis=2, tiled=True)
    )
    d_hidden = mix_columns(
        lax.all_to_all(spread(d_result), "seq", split_axis=2, concat_axis=1, tiled=True)
    )
    d_second = (d_hidden * kernel).astype(bf16)
    d_inputs = finish_rows(
        lax.all_to_all(unmix_columns(d_second), "seq", split_axis=1, concat_axis=2, tiled=True)
    )
    mixed = (result * gate32).astype(bf16)
    grad_gate = (cot * result).astype(bf16)
    grad_inputs = d_inputs.astype(bf16)
    grad_kernel = lax.psum(jnp.sum(d_hidden * second, axis=0), "dp")
    return (mixed, grad_inputs, grad_gate, grad_kernel)


def solution(mesh):
    placed = (
        P("dp", "seq", None, None),
        P("dp", "seq", None, None),
        P(None, "seq", None),
        P("seq", None, None),
        P("seq", None, None),
        P("dp", "seq", None, None),
    )
    return jax.shard_map(
        shards,
        mesh=mesh,
        in_specs=placed,
        out_specs=(
            P("dp", "seq", None, None),
            P("dp", "seq", None, None),
            P("dp", "seq", None, None),
            P(None, "seq", None),
        ),
        check_vma=False,
    )
```

profile of v0, /device:TPU:1, one launch (start us, length us, event | category | flops | bytes accessed | tf_op | source)
XLA Modules:
  0.0 193.4 jit_solution(5639259495040109000)
XLA Ops:
  7.2 1.0 copy-done
  8.2 1.3 fusion
  9.5 1.2 copy.43
  10.7 14.0 %all-to-all-start = ((bf16[1,2,256,512]{3,1,0,2:T(2,128)(2,1)}), bf16[1,2,256,512]{3,1,0,2:T(2,128)(2,1)S(1)}, u32[]{:S(2)}, u32[]{:S(2)}) async-start(bf16[1,2,256,512]{3,1,0,2:T(2,128)(2,1)} %copy.43), calls=%async_computation | async-start | bytes 1048576 | tf_op jit(solution)/shard_map/all_to_all | solution.py:31
  24.9 0.8 copy-done.11
  25.9 0.7 copy-done.6
  27.0 0.4 copy-done.1
  27.5 1.2 copy.52
  28.6 14.2 %all-to-all-done = bf16[1,2,256,512]{3,1,0,2:T(2,128)(2,1)S(1)} async-done(((bf16[1,2,256,512]{3,1,0,2:T(2,128)(2,1)}), bf16[1,2,256,512]{3,1,0,2:T(2,128)(2,1)S(1)}, u32[]{:S(2)}, u32[]{:S(2)}) %all-to-all-start) | async-done | bytes 524320 | tf_op jit(solution)/shard_map/all_to_all | solution.py:31
  42.8 0.8 copy-done.8
  43.6 6.9 %all-to-all-start.2 = ((bf16[1,2,256,512]{3,1,0,2:T(2,128)(2,1)}), bf16[1,2,256,512]{3,1,0,2:T(2,128)(2,1)S(1)}, u32[]{:S(2)}, u32[]{:S(2)}) async-start(bf16[1,2,256,512]{3,1,0,2:T(2,128)(2,1)} %copy.52), calls=%async_computation.2 | async-start | bytes 1048576 | tf_op jit(solution)/shard_map/all_to_all | solution.py:38
  50.6 0.5 copy.46
  51.1 0.5 copy-done.9
  52.0 0.5 copy-done.5
  52.9 1.1 fusion.1
  54.0 2.0 %copy.47 = bf16[1,256,2,512]{3,2,0,1:T(2,128)(2,1)} copy(bf16[1,256,2,512]{1,3,2,0:T(8,128)(2,1)} %fusion.1) | data formatting | bytes 1048576 | tf_op jit(solution)/shard_map/convert_element_type | solution.py:25
  56.0 12.7 %all-to-all-done.2 = bf16[1,2,256,512]{3,1,0,2:T(2,128)(2,1)S(1)} async-done(((bf16[1,2,256,512]{3,1,0,2:T(2,128)(2,1)}), bf16[1,2,256,512]{3,1,0,2:T(2,128)(2,1)S(1)}, u32[]{:S(2)}, u32[]{:S(2)}) %all-to-all-start.2) | async-done | bytes 524320 | tf_op jit(solution)/shard_map/all_to_all | solution.py:38
  68.7 7.5 %all-to-all-start.1 = ((bf16[1,256,2,512]{3,2,0,1:T(2,128)(2,1)}), bf16[1,256,2,512]{3,2,0,1:T(2,128)(2,1)}, u32[]{:S(2)}, u32[]{:S(2)}) async-start(bf16[1,256,2,512]{3,2,0,1:T(2,128)(2,1)} %copy.47), calls=%async_computation.1 | async-start | bytes 1048576 | tf_op jit(solution)/shard_map/all_to_all | solution.py:35
  77.0 0.7 copy-done.4
  77.7 1.1 fusion.3
  78.8 2.0 %copy.55 = bf16[1,256,2,512]{3,2,0,1:T(2,128)(2,1)} copy(bf16[1,256,2,512]{1,3,2,0:T(8,128)(2,1)} %fusion.3) | data formatting | bytes 1048576 | tf_op jit(solution)/shard_map/convert_element_type | solution.py:25
  80.8 13.4 %all-to-all-done.1 = bf16[1,256,2,512]{3,2,0,1:T(2,128)(2,1)} async-done(((bf16[1,256,2,512]{3,2,0,1:T(2,128)(2,1)}), bf16[1,256,2,512]{3,2,0,1:T(2,128)(2,1)}, u32[]{:S(2)}, u32[]{:S(2)}) %all-to-all-start.1) | async-done | bytes 524320 | tf_op jit(solution)/shard_map/all_to_all | solution.py:35
  94.1 7.7 %all-to-all-start.3 = ((bf16[1,256,2,512]{3,2,0,1:T(2,128)(2,1)}), bf16[1,256,2,512]{3,2,0,1:T(2,128)(2,1)}, u32[]{:S(2)}, u32[]{:S(2)}) async-start(bf16[1,256,2,512]{3,2,0,1:T(2,128)(2,1)} %copy.55), calls=%async_computation.3 | async-start | bytes 1048576 | tf_op jit(solution)/shard_map/all_to_all | solution.py:42
  101.8 1.1 multiply_bitcast_fusion
  103.0 1.5 copy.48
  104.9 1.0 copy.58
  105.9 13.8 %all-to-all-done.3 = bf16[1,256,2,512]{3,2,0,1:T(2,128)(2,1)} async-done(((bf16[1,256,2,512]{3,2,0,1:T(2,128)(2,1)}), bf16[1,256,2,512]{3,2,0,1:T(2,128)(2,1)}, u32[]{:S(2)}, u32[]{:S(2)}) %all-to-all-start.3) | async-done | bytes 524320 | tf_op jit(solution)/shard_map/all_to_all | solution.py:42
  119.7 1.5 copy.56
  121.5 1.0 copy.59
  122.5 1.0 copy.60
  123.5 60.8 %all-reduce.2.cloned.1.call-done = f32[256,2,512]{0,2,1:T(8,128)} async-done(((f32[256,2,512]{0,2,1:T(8,128)}), f32[256,2,512]{0,2,1:T(8,128)}) %all-reduce.2.cloned.1.call-update) | async-done | bytes 1048592 | tf_op jit(solution)/shard_map/psum | solution.py:47
  184.3 2.2 %copy.61 = f32[256,2,512]{2,1,0:T(2,128)} copy(f32[256,2,512]{0,2,1:T(8,128)} %all-reduce.2.cloned.1.call-done) | data formatting | bytes 2097152
  (29 shorter events, 3.1 us)
Async XLA Ops:
  7.2 1.0 copy-start
  10.7 14.0 %copy-start.10 = (bf16[1,2,256,512]{3,2,1,0:T(8,128)(2,1)S(1)}, bf16[1,2,256,512]{3,2,1,0:T(8,128)(2,1)}, u32[]{:S(2)}) copy-start(bf16[1,2,256,512]{3,2,1,0:T(8,128)(2,1)} %param.11) | copy-start | bytes 1572868
  10.7 32.1 %all-to-all-start = ((bf16[1,2,256,512]{3,1,0,2:T(2,128)(2,1)}), bf16[1,2,256,512]{3,1,0,2:T(2,128)(2,1)S(1)}, u32[]{:S(2)}, u32[]{:S(2)}) async-start(bf16[1,2,256,512]{3,1,0,2:T(2,128)(2,1)} %copy.43), calls=%async_computation | async-start | bytes 1048576 | tf_op jit(solution)/shard_map/all_to_all | solution.py:31
  24.7 1.0 copy-start.11
  25.7 0.9 copy-start.6
  26.7 0.8 copy-start.1
  28.6 21.9 %copy-start.12 = (bf16[256,2,512]{2,1,0:T(2,128)(2,1)S(1)}, bf16[256,2,512]{2,1,0:T(2,128)(2,1)}, u32[]{:S(2)}) copy-start(bf16[256,2,512]{2,1,0:T(2,128)(2,1)} %param.8) | copy-start | bytes 1572868
  42.8 0.8 copy-start.8
  43.6 25.1 %all-to-all-start.2 = ((bf16[1,2,256,512]{3,1,0,2:T(2,128)(2,1)}), bf16[1,2,256,512]{3,1,0,2:T(2,128)(2,1)S(1)}, u32[]{:S(2)}, u32[]{:S(2)}) async-start(bf16[1,2,256,512]{3,1,0,2:T(2,128)(2,1)} %copy.52), calls=%async_computation.2 | async-start | bytes 1048576 | tf_op jit(solution)/shard_map/all_to_all | solution.py:38
  50.6 1.0 copy-start.9
  51.1 1.8 copy-start.3
  51.6 0.9 copy-start.5
  68.7 25.4 %all-to-all-start.1 = ((bf16[1,256,2,512]{3,2,0,1:T(2,128)(2,1)}), bf16[1,256,2,512]{3,2,0,1:T(2,128)(2,1)}, u32[]{:S(2)}, u32[]{:S(2)}) async-start(bf16[1,256,2,512]{3,2,0,1:T(2,128)(2,1)} %copy.47), calls=%async_computation.1 | async-start | bytes 1048576 | tf_op jit(solution)/shard_map/all_to_all | solution.py:35
  76.6 1.0 copy-start.4
  94.1 25.6 %all-to-all-start.3 = ((bf16[1,256,2,512]{3,2,0,1:T(2,128)(2,1)}), bf16[1,256,2,512]{3,2,0,1:T(2,128)(2,1)}, u32[]{:S(2)}, u32[]{:S(2)}) async-start(bf16[1,256,2,512]{3,2,0,1:T(2,128)(2,1)} %copy.55), calls=%async_computation.3 | async-start | bytes 1048576 | tf_op jit(solution)/shard_map/all_to_all | solution.py:42
  101.8 82.6 %all-reduce.2.cloned.1.call-start = ((), (), s32[]{:S(2)}) async-start(), calls=%async_computation.4 | async-start | bytes 2097152 | tf_op jit(solution)/shard_map/psum | solution.py:47
  103.0 1.6 copy-start.2
  103.0 1.6 copy-start.7
Sparse Core Ops, SparseCore 0:
  105.8 78.5 all-reduce.1
where the time goes:
time: 194 us; the launch traced here: 193 us
  waiting for transfers between devices  115 us (59%)
  starting transfers between devices  36.1 us (19%)
  local copies, waits for them, and re-layouts  21.9 us (11%)
  between operations  14.2 us (7%)
  matrix products  5.23 us (3%)
    psum x1, waiting for transfers between devices, shards(): grad_kernel = lax.psum(jnp.sum(d_hidden * second, axis=0), 'dp')  60.8 us
    all_to_all x1, waiting for transfers between devices, shards(): lax.all_to_all(spread(inputs), 'seq', split_axis=2, concat_axis=1, tiled=...  14.2 us
    all_to_all x1, starting transfers between devices, shards(): lax.all_to_all(spread(inputs), 'seq', split_axis=2, concat_axis=1, tiled=...  14 us
    all_to_all x1, waiting for transfers between devices, shards(): lax.all_to_all(unmix_columns(d_second), 'seq', split_axis=1, concat_axis=...  13.8 us
    all_to_all x1, waiting for transfers between devices, shards(): lax.all_to_all(unmix_columns(hidden), 'seq', split_axis=1, concat_axis=2,...  13.4 us
    all_to_all x1, waiting for transfers between devices, shards(): lax.all_to_all(spread(d_result), 'seq', split_axis=2, concat_axis=1, tile...  12.7 us
    unnamed x33, local copies, waits for them, and re-layouts  11.8 us
    all_to_all x1, starting transfers between devices, shards(): lax.all_to_all(unmix_columns(d_second), 'seq', split_axis=1, concat_axis=...  7.66 us
  transfers between devices with their start and end apart: 5, of which 5 were waited for; matrix products, arithmetic and copies ran while one was open for 9% of the time, Pallas kernels for 0%

commit v1 on v0

--- a/solution.py
+++ b/solution.py
@@ -2,6 +2,7 @@
 import jax.numpy as jnp
 from jax import lax
 from jax.sharding import PartitionSpec as P
+from jax.lax import all_gather
 
 
 def shards(inputs, gate, kernel, first_blocks, second_blocks, cotangent):
@@ -44,7 +45,12 @@
     mixed = (result * gate32).astype(bf16)
     grad_gate = (cot * result).astype(bf16)
     grad_inputs = d_inputs.astype(bf16)
-    grad_kernel = lax.psum(jnp.sum(d_hidden * second, axis=0), "dp")
+
+    def _carry_sectors(message, lane_axis):
+        x_new = all_gather(message, lane_axis).sum(axis=0)
+        return x_new
+
+    grad_kernel = _carry_sectors(jnp.sum(d_hidden * second, axis=0), "dp")
     return (mixed, grad_inputs, grad_gate, grad_kernel)
 
 

time: 194 us -> 179 us (0.923)
  waiting for transfers between devices: 115 us -> 96 us
  matrix products: 5.23 us -> 9.57 us
    psum x1 -> x0, waiting for transfers between devices: 60.8 us -> none  [shards(): grad_kernel = lax.psum(jnp.sum(d_hidden * second, axis=0), 'dp')]
    all_to_all x1, waiting for transfers between devices: 13.8 us -> 55.3 us  [shards(): lax.all_to_all(unmix_columns(d_second), 'seq', split_axis=1, concat_axis=...]
    all_to_all x1, starting transfers between devices: 14 us -> 6.93 us  [shards(): lax.all_to_all(spread(inputs), 'seq', split_axis=2, concat_axis=1, tiled=...]
    all_to_all x1, starting transfers between devices: 6.93 us -> 13.8 us  [shards(): lax.all_to_all(spread(d_result), 'seq', split_axis=2, concat_axis=1, tile...]
    all_to_all x1, waiting for transfers between devices: 13.4 us -> 8.39 us  [shards(): lax.all_to_all(unmix_columns(hidden), 'seq', split_axis=1, concat_axis=2,...]
    all_to_all x1, waiting for transfers between devices: 12.7 us -> 16.6 us  [shards(): lax.all_to_all(spread(d_result), 'seq', split_axis=2, concat_axis=1, tile...]
    dot_general x2, matrix products: 0.69 us -> 4.07 us  [mix_columns(): jnp.einsum('cqr,srcd->sqcd', second_blocks, piece, preferred_element_type...]
    unnamed x33 -> x13, local copies, waits for them, and re-layouts: 11.8 us -> 8.66 us
  transfers between devices with their start and end apart: 5 -> 5, of which waited for: 5 -> 4; matrix products, arithmetic and copies ran while one was open for 9% -> 11% of each run, Pallas kernels for 0% -> 0%
where the time goes in v1:
time: 179 us; the launch traced here: 178 us
  waiting for transfers between devices  96 us (54%)
  starting transfers between devices  35.2 us (20%)
  local copies, waits for them, and re-layouts  21.1 us (12%)
  between operations  14.2 us (8%)
  matrix products  9.57 us (5%)
  other arithmetic  1.9 us (1%)
    all_to_all x1, waiting for transfers between devices, shards(): lax.all_to_all(unmix_columns(d_second), 'seq', split_axis=1, concat_axis=...  55.3 us
    all_to_all x1, waiting for transfers between devices, shards(): lax.all_to_all(spread(d_result), 'seq', split_axis=2, concat_axis=1, tile...  16.6 us
    all_to_all x1, waiting for transfers between devices, shards(): lax.all_to_all(spread(inputs), 'seq', split_axis=2, concat_axis=1, tiled=...  15.6 us
    all_to_all x1, starting transfers between devices, shards(): lax.all_to_all(spread(d_result), 'seq', split_axis=2, concat_axis=1, tile...  13.8 us
    unnamed x13, local copies, waits for them, and re-layouts  8.66 us
    all_to_all x1, waiting for transfers between devices, shards(): lax.all_to_all(unmix_columns(hidden), 'seq', split_axis=1, concat_axis=2,...  8.39 us
    all_to_all x1, starting transfers between devices, shards(): lax.all_to_all(unmix_columns(hidden), 'seq', split_axis=1, concat_axis=2,...  7.48 us
    all_to_all x1, starting transfers between devices, shards(): lax.all_to_all(spread(inputs), 'seq', split_axis=2, concat_axis=1, tiled=...  6.93 us
  transfers between devices with their start and end apart: 5, of which 4 were waited for; matrix products, arithmetic and copies ran while one was open for 11% of the time, Pallas kernels for 0%

profile of v1, /device:TPU:1, one launch (start us, length us, event | category | flops | bytes accessed | tf_op | source)
XLA Modules:
  0.0 178.0 jit_solution(5469219848976568522)
XLA Ops:
  7.2 1.3 copy.48
  8.5 1.2 copy.49
  9.8 0.3 fusion.2
  10.1 1.2 copy.50
  11.3 13.8 %all-to-all-start.2 = ((bf16[1,2,256,512]{3,1,0,2:T(2,128)(2,1)}), bf16[1,2,256,512]{3,1,0,2:T(2,128)(2,1)S(1)}, u32[]{:S(2)}, u32[]{:S(2)}) async-start(bf16[1,2,256,512]{3,1,0,2:T(2,128)(2,1)} %copy.50), calls=%async_computation.2 | async-start | bytes 1048576 | tf_op jit(solution)/shard_map/all_to_all | solution.py:39
  25.1 0.3 fusion
  25.5 1.2 copy.41
  26.7 16.6 %all-to-all-done.2 = bf16[1,2,256,512]{3,1,0,2:T(2,128)(2,1)S(1)} async-done(((bf16[1,2,256,512]{3,1,0,2:T(2,128)(2,1)}), bf16[1,2,256,512]{3,1,0,2:T(2,128)(2,1)S(1)}, u32[]{:S(2)}, u32[]{:S(2)}) %all-to-all-start.2) | async-done | bytes 524320 | tf_op jit(solution)/shard_map/all_to_all | solution.py:39
  43.3 6.9 %all-to-all-start = ((bf16[1,2,256,512]{3,1,0,2:T(2,128)(2,1)}), bf16[1,2,256,512]{3,1,0,2:T(2,128)(2,1)S(1)}, u32[]{:S(2)}, u32[]{:S(2)}) async-start(bf16[1,2,256,512]{3,1,0,2:T(2,128)(2,1)} %copy.41), calls=%async_computation | async-start | bytes 1048576 | tf_op jit(solution)/shard_map/all_to_all | solution.py:32
  50.2 1.3 copy.44
  51.5 1.2 copy.51
  52.7 15.6 %all-to-all-done = bf16[1,2,256,512]{3,1,0,2:T(2,128)(2,1)S(1)} async-done(((bf16[1,2,256,512]{3,1,0,2:T(2,128)(2,1)}), bf16[1,2,256,512]{3,1,0,2:T(2,128)(2,1)S(1)}, u32[]{:S(2)}, u32[]{:S(2)}) %all-to-all-start) | async-done | bytes 524320 | tf_op jit(solution)/shard_map/all_to_all | solution.py:32
  68.4 0.4 copy.42
  68.8 1.3 convolution_bitcast_fusion.2
  70.1 2.0 %fusion.1 = bf16[1,256,2,512]{1,3,2,0:T(8,128)(2,1)} fusion(bf16[2,256,256]{2,1,0:T(8,128)(2,1)} %param.10, f32[1,256,2,512]{1,3,2,0:T(8,128)S(1)} %convolution_bitcast_fusion.2, bf16[256,2,512]{0,2,1:T(8,128)(2,1)S(1)} %copy.44), kind=kOutput, calls=%fused_computation.14 | convolution fusion | flops 135266304 | bytes 2359296 | tf_op jit(solution)/shard_map/cqr,sqcd->srcd/dot_general | solution.py:24
  72.1 2.0 %copy.45 = bf16[1,256,2,512]{3,2,0,1:T(2,128)(2,1)} copy(bf16[1,256,2,512]{1,3,2,0:T(8,128)(2,1)} %fusion.1) | data formatting | bytes 1048576 | tf_op jit(solution)/shard_map/convert_element_type | solution.py:26
  74.2 7.5 %all-to-all-start.1 = ((bf16[1,256,2,512]{3,2,0,1:T(2,128)(2,1)}), bf16[1,256,2,512]{3,2,0,1:T(2,128)(2,1)}, u32[]{:S(2)}, u32[]{:S(2)}) async-start(bf16[1,256,2,512]{3,2,0,1:T(2,128)(2,1)} %copy.45), calls=%async_computation.1 | async-start | bytes 1048576 | tf_op jit(solution)/shard_map/all_to_all | solution.py:36
  81.7 2.8 %fusion.23 = (f32[1,256,2,512]{1,3,2,0:T(8,128)}, f32[1,256,2,512]{1,3,2,0:T(8,128)}) fusion(f32[1,256,2,512]{1,3,2,0:T(8,128)S(1)} %convolution_bitcast_fusion.2, bf16[2,256,256]{2,1,0:T(8,128)(2,1)} %param.10, bf16[256,2,512]{2,1,0:T(2,128)(2,1)} %bitcast.78), kind=kOutput, calls=%fused_computation.33 | convolution fusion | flops 134479872 | bytes 3932160 | tf_op jit(solution)/shard_map/cqr,srcd->sqcd/dot_general | solution.py:21
  84.5 2.6 %copy.56 = f32[1,256,2,512]{3,1,2,0:T(8,128)} copy(f32[1,256,2,512]{1,3,2,0:T(8,128)} %get-tuple-element.18) | data formatting | bytes 2097152 | tf_op jit(solution)/shard_map/mul | solution.py:53
  87.1 2.0 %fusion.3 = bf16[1,256,2,512]{1,3,2,0:T(8,128)(2,1)} fusion(bf16[2,256,256]{2,1,0:T(8,128)(2,1)} %param.10, f32[1,256,2,512]{1,3,2,0:T(8,128)S(1)} %copy-done.2, bf16[256,2,512]{0,2,1:T(8,128)(2,1)S(1)} %copy.44), kind=kOutput, calls=%fused_computation.16 | convolution fusion | flops 135266304 | bytes 2359296 | tf_op jit(solution)/shard_map/cqr,sqcd->srcd/dot_general | solution.py:24
  89.2 2.0 %copy.53 = bf16[1,256,2,512]{3,2,0,1:T(2,128)(2,1)} copy(bf16[1,256,2,512]{1,3,2,0:T(8,128)(2,1)} %fusion.3) | data formatting | bytes 1048576 | tf_op jit(solution)/shard_map/convert_element_type | solution.py:26
  91.2 8.4 %all-to-all-done.1 = bf16[1,256,2,512]{3,2,0,1:T(2,128)(2,1)} async-done(((bf16[1,256,2,512]{3,2,0,1:T(2,128)(2,1)}), bf16[1,256,2,512]{3,2,0,1:T(2,128)(2,1)}, u32[]{:S(2)}, u32[]{:S(2)}) %all-to-all-start.1) | async-done | bytes 524320 | tf_op jit(solution)/shard_map/all_to_all | solution.py:36
  99.6 6.9 %all-to-all-start.3 = ((bf16[1,256,2,512]{3,2,0,1:T(2,128)(2,1)}), bf16[1,256,2,512]{3,2,0,1:T(2,128)(2,1)S(1)}, u32[]{:S(2)}, u32[]{:S(2)}) async-start(bf16[1,256,2,512]{3,2,0,1:T(2,128)(2,1)} %copy.53), calls=%async_computation.3 | async-start | bytes 1048576 | tf_op jit(solution)/shard_map/all_to_all | solution.py:43
  106.5 1.5 copy.46
  108.0 0.4 fusion.7
  108.3 1.0 copy.60
  109.3 1.0 copy.58
  110.4 55.3 %all-to-all-done.3 = bf16[1,256,2,512]{3,2,0,1:T(2,128)(2,1)S(1)} async-done(((bf16[1,256,2,512]{3,2,0,1:T(2,128)(2,1)}), bf16[1,256,2,512]{3,2,0,1:T(2,128)(2,1)S(1)}, u32[]{:S(2)}, u32[]{:S(2)}) %all-to-all-start.3) | async-done | bytes 524320 | tf_op jit(solution)/shard_map/all_to_all | solution.py:43
  165.7 0.4 copy.54
  166.5 1.0 copy.59
  167.5 1.9 %reduce_sum.8 = f32[256,2,512]{2,0,1:T(8,128)S(1)} reduce(f32[2,256,2,512]{3,1,2,0:T(8,128)} %all-gather.2.cloned.1.call-done, f32[]{:T(128)} %constant.0.clone.1), dimensions={0}, to_apply=%region_0.0 | reduce | flops 262144 | bytes 3145732 | tf_op jit(solution)/shard_map/reduce_sum | solution.py:50
  169.4 1.8 %copy.61 = f32[256,2,512]{2,1,0:T(2,128)} copy(f32[256,2,512]{2,0,1:T(8,128)S(1)} %reduce_sum.8) | data formatting | bytes 2097152
  (10 shorter events, 0.4 us)
Async XLA Ops:
  7.2 18.0 %copy-start = (bf16[1,2,256,512]{3,2,1,0:T(8,128)(2,1)S(1)}, bf16[1,2,256,512]{3,2,1,0:T(8,128)(2,1)}, u32[]{:S(2)}) copy-start(bf16[1,2,256,512]{3,2,1,0:T(8,128)(2,1)} %param.6) | copy-start | bytes 1572868
  7.2 2.6 %copy-start.1 = (bf16[2,256,256]{2,1,0:T(8,128)(2,1)S(1)}, bf16[2,256,256]{2,1,0:T(8,128)(2,1)}, u32[]{:S(2)}) copy-start(bf16[2,256,256]{2,1,0:T(8,128)(2,1)} %param.9) | copy-start | bytes 786436
  11.3 32.0 %all-to-all-start.2 = ((bf16[1,2,256,512]{3,1,0,2:T(2,128)(2,1)}), bf16[1,2,256,512]{3,1,0,2:T(2,128)(2,1)S(1)}, u32[]{:S(2)}, u32[]{:S(2)}) async-start(bf16[1,2,256,512]{3,1,0,2:T(2,128)(2,1)} %copy.50), calls=%async_computation.2 | async-start | bytes 1048576 | tf_op jit(solution)/shard_map/all_to_all | solution.py:39
  43.3 25.1 %all-to-all-start = ((bf16[1,2,256,512]{3,1,0,2:T(2,128)(2,1)}), bf16[1,2,256,512]{3,1,0,2:T(2,128)(2,1)S(1)}, u32[]{:S(2)}, u32[]{:S(2)}) async-start(bf16[1,2,256,512]{3,1,0,2:T(2,128)(2,1)} %copy.41), calls=%async_computation | async-start | bytes 1048576 | tf_op jit(solution)/shard_map/all_to_all | solution.py:32
  74.2 25.4 %all-to-all-start.1 = ((bf16[1,256,2,512]{3,2,0,1:T(2,128)(2,1)}), bf16[1,256,2,512]{3,2,0,1:T(2,128)(2,1)}, u32[]{:S(2)}, u32[]{:S(2)}) async-start(bf16[1,256,2,512]{3,2,0,1:T(2,128)(2,1)} %copy.45), calls=%async_computation.1 | async-start | bytes 1048576 | tf_op jit(solution)/shard_map/all_to_all | solution.py:36
  81.6 85.8 %all-gather.2.cloned.1.call-start = ((), (), s32[]{:S(2)}) async-start(), calls=%async_computation.4 | async-start | bytes 3145728 | tf_op jit(solution)/shard_map/all_gather | solution.py:50
  84.5 2.6 %copy-start.2 = (f32[1,256,2,512]{1,3,2,0:T(8,128)S(1)}, f32[1,256,2,512]{1,3,2,0:T(8,128)}, u32[]{:S(2)}) copy-start(f32[1,256,2,512]{1,3,2,0:T(8,128)} %get-tuple-element.19) | copy-start | bytes 3145732
  99.6 66.1 %all-to-all-start.3 = ((bf16[1,256,2,512]{3,2,0,1:T(2,128)(2,1)}), bf16[1,256,2,512]{3,2,0,1:T(2,128)(2,1)S(1)}, u32[]{:S(2)}, u32[]{:S(2)}) async-start(bf16[1,256,2,512]{3,2,0,1:T(2,128)(2,1)} %copy.53), calls=%async_computation.3 | async-start | bytes 1048576 | tf_op jit(solution)/shard_map/all_to_all | solution.py:43
Sparse Core Ops, SparseCore 0:
  87.2 73.6 all-gather.1
